TPU v7x, 128 devices: a whole 4x4x4 slice. The times are simulated.
128 devices in a mesh: replica: 8 (over z, y_lo), fsdp: 16 (over y_hi, x, core).
Axes of the slice: x: 4, y: 4 (y_hi: 2, y_lo: 2; y = y_hi * 2 + y_lo), z: 4, core: 2. Of those that a mesh axis runs over, the one named last changes fastest.
Arguments:
- tokens: bfloat16 [8, 2048, 4096], P('replica', 'fsdp'), may hold values from -6 to 6
- queries: bfloat16 [8, 2048, 4096], P('replica', 'fsdp'), may hold values from -64 to 64
- keys: bfloat16 [8, 2048, 512], P('replica', 'fsdp'), may hold values from -4 to 4
- value_weight: bfloat16 [4096, 512], P('fsdp'), may hold values from -4 to 4
- ctx_grad: bfloat16 [8, 2048, 4096], P('replica', 'fsdp'), may hold values from -6 to 6
- frag_global: float32 [4096, 2048], P('fsdp', 'replica'), may hold values from -4 to 4
- frag_momentum: float32 [4096, 2048], P('fsdp', 'replica'), may hold values from -1.8 to 1.8
- frag_local: bfloat16 [8, 4096, 2048], P('replica', 'fsdp'), may hold values from -6 to 6
Outputs:
- context: bfloat16 [8, 2048, 4096], P('replica', 'fsdp')
- query_grad: bfloat16 [8, 2048, 4096], P('replica', 'fsdp')
- key_grad: bfloat16 [8, 2048, 512], P('replica', 'fsdp')
- weight_grad: float32 [8, 4096, 512], P('replica', 'fsdp')
- token_grad: bfloat16 [8, 2048, 4096], P('replica', 'fsdp')
- new_global: float32 [4096, 2048], P('fsdp', 'replica')
- new_momentum: float32 [4096, 2048], P('fsdp', 'replica')
- refreshed_local: bfloat16 [4096, 2048], P('fsdp')
All inputs are finite; a program needn't handle non-finite values.
Results may differ from a plain program's by a relative error of at most 0.02.
Values may be sent and summed in bfloat16 or wider, within the bound.
No kernel may reach another device: no remote copies, remote signals or barrier semaphores. Data moves between devices by JAX's collectives and lax.ppermute only.
A program may use at most 192 MiB of HBM per device.

v0:
```python
import jax
import jax.numpy as jnp
from jax import lax
from jax.sharding import PartitionSpec as P

HD = 128


outer_momentum = 0.9
outer_rate = 0.7
masked_score = -1e30


def on_device(
    tokens, queries, keys, value_weight, ctx_grad, frag_global, frag_momentum, frag_local
):
    tokens = tokens[0]
    queries = queries[0]
    keys = keys[0]
    ctx_grad = ctx_grad[0]
    tok_rows = tokens.shape[0]
    model_width = tokens.shape[1]
    proj_scale = model_width ** (-0.5)
    score_scale = HD ** (-0.5)
    kv_heads = keys.shape[1] // HD
    group = queries.shape[1] // (kv_heads * HD)
    columns = tokens
    value_sum = jnp.dot(
        columns,
        lax.all_gather(value_weight, "fsdp", axis=0, tiled=True),
        preferred_element_type=jnp.float32,
    )
    values = (value_sum * proj_scale).astype(jnp.bfloat16)
    keys_all, values_all = (
        lax.all_gather(keys, "fsdp", axis=0, tiled=True),
        lax.all_gather(values, "fsdp", axis=0, tiled=True),
    )
    length_all = keys_all.shape[0]
    query_pos = lax.axis_index("fsdp") * tok_rows + jnp.arange(tok_rows)
    causal = jnp.arange(length_all)[None, :] <= query_pos[:, None]
    query_heads = queries.reshape(tok_rows, kv_heads, group, HD)
    grad_heads = ctx_grad.reshape(tok_rows, kv_heads, group, HD)
    context_list = []
    query_list = []
    key_terms = []
    value_terms = []
    for group_index in range(kv_heads):
        query_part = query_heads[:, group_index]
        grad_part = grad_heads[:, group_index]
        key_part = keys_all[:, group_index * HD : (group_index + 1) * HD]
        value_part = values_all[:, group_index * HD : (group_index + 1) * HD]
        scores = (
            jnp.einsum("thd,kd->htk", query_part, key_part, preferred_element_type=jnp.float32)
            * score_scale
        )
        scores = jnp.where(causal[None], scores, masked_score)
        top = jnp.max(scores, axis=-1, keepdims=True)
        summed = jnp.sum(jnp.exp(scores - top), axis=-1, keepdims=True)
        log_total = top + jnp.log(summed)
        probs = jnp.exp(scores - log_total)
        probs_low = probs.astype(jnp.bfloat16)
        context_part = jnp.einsum(
            "htk,kd->thd", probs_low, value_part, preferred_element_type=jnp.float32
        ).astype(jnp.bfloat16)
        dprobs = jnp.einsum(
            "thd,kd->htk", grad_part, value_part, preferred_element_type=jnp.float32
        )
        rowdot = jnp.sum(
            grad_part.astype(jnp.float32) * context_part.astype(jnp.float32), axis=-1
        ).transpose(1, 0)[:, :, None]
        dscores = (probs * (dprobs - rowdot) * score_scale).astype(jnp.bfloat16)
        query_list.append(
            jnp.einsum("htk,kd->thd", dscores, key_part, preferred_element_type=jnp.float32).astype(
                jnp.bfloat16
            )
        )
        key_terms.append(
            jnp.einsum("htk,thd->kd", dscores, query_part, preferred_element_type=jnp.float32)
        )
        value_terms.append(
            jnp.einsum("htk,thd->kd", probs_low, grad_part, preferred_element_type=jnp.float32)
        )
        context_list.append(context_part)
    context = jnp.stack(context_list, axis=1).reshape(tok_rows, queries.shape[1])
    query_grad = jnp.stack(query_list, axis=1).reshape(tok_rows, queries.shape[1])
    key_term = jnp.concatenate(key_terms, axis=1)
    value_term = jnp.concatenate(value_terms, axis=1)
    key_sum, value_total = (
        lax.psum_scatter(
            key_term.astype(jnp.bfloat16), "fsdp", scatter_dimension=0, tiled=True
        ).astype(jnp.float32),
        lax.psum_scatter(
            value_term.astype(jnp.bfloat16), "fsdp", scatter_dimension=0, tiled=True
        ).astype(jnp.float32),
    )
    key_grad = key_sum.astype(jnp.bfloat16)
    value_grad = value_total.astype(jnp.bfloat16)
    columns = tokens
    product = lax.dot_general(
        columns, value_grad, (((0,), (0,)), ((), ())), preferred_element_type=jnp.float32
    )
    weight_grad = lax.psum_scatter(
        (product * proj_scale).astype(jnp.bfloat16), "fsdp", scatter_dimension=0, tiled=True
    ).astype(jnp.float32)
    token_sum = lax.dot_general(
        value_grad,
        lax.all_gather(value_weight, "fsdp", axis=0, tiled=True),
        (((1,), (1,)), ((), ())),
        preferred_element_type=jnp.float32,
    )
    token_grad = (token_sum * proj_scale).astype(jnp.bfloat16)
    replicas = lax.axis_size("replica")
    local_term = frag_local[0].astype(jnp.float32)
    summed_frag = lax.psum(local_term, "replica")
    share_cols = frag_global.shape[1]
    own_sum = lax.dynamic_slice_in_dim(
        summed_frag, lax.axis_index("replica") * share_cols, share_cols, 1
    )
    delta = frag_global - own_sum / replicas
    new_momentum = outer_momentum * frag_momentum + delta
    new_global = frag_global - outer_rate * (delta + outer_momentum * new_momentum)
    refreshed_local = lax.all_gather(new_global.astype(jnp.bfloat16), "replica", axis=1, tiled=True)
    return (
        context[None],
        query_grad[None],
        key_grad[None],
        weight_grad[None],
        token_grad[None],
        new_global,
        new_momentum,
        refreshed_local,
    )


def solution(mesh):
    return jax.shard_map(
        on_device,
        mesh=mesh,
        in_specs=(
            P("replica", "fsdp", None),
            P("replica", "fsdp", None),
            P("replica", "fsdp", None),
            P("fsdp", None),
            P("replica", "fsdp", None),
            P("fsdp", "replica"),
            P("fsdp", "replica"),
            P("replica", "fsdp", None),
        ),
        out_specs=(
            P("replica", "fsdp", None),
            P("replica", "fsdp", None),
            P("replica", "fsdp", None),
            P("replica", "fsdp", None),
            P("replica", "fsdp", None),
            P("fsdp", "replica"),
            P("fsdp", "replica"),
            P("fsdp", None),
        ),
        check_vma=False,
    )
```

profile of v0, /device:TPU:1, one launch (start us, length us, event | category | flops | bytes accessed | tf_op | source)
XLA Modules:
  0.0 464.1 jit_solution(7964945165910970632)
XLA Ops:
  9.6 2.8 bitcast_convert_fusion
  15.7 53.3 %all-gather.12.cloned.1.call-done = bf16[1,2048,512]{2,1,0:T(8,128)(2,1)} async-done(((bf16[1,128,512]{2,1,0:T(8,128)(2,1)}), bf16[1,2048,512]{2,1,0:T(8,128)(2,1)}) %all-gather.12.cloned.1.call-update) | async-done | bytes 2097168 | tf_op jit(solution)/shard_map/all_gather | solution.py:35
  69.0 2.4 fusion.40
  72.7 5.1 %fusion.17 = (f32[8,128]{1,0:T(8,128)S(1)}, f32[2048,128,8]{1,0,2:T(8,128)}) fusion(pred[128,2048]{0,1:T(8,128)(4,1)S(1)} %iota_compare_fusion, bf16[128,4,8,128]{0,3,2,1:T(8,128)(2,1)S(1)} %bitcast.293, bf16[2048,512]{1,0:T(8,128)(2,1)S(1)} %bitcast.313), kind=kOutput, calls=%fused_computation.34 | convolution fusion | flops 543161344 | bytes 9441280 | tf_op jit(solution)/shard_map/thd,kd->htk/dot_general | solution.py:53
  77.8 11.4 %exponential_reduce_fusion.3 = (f32[8,128]{1,0:T(8,128)S(1)}, f32[8,128]{1,0:T(8,128)S(1)}, f32[8,128]{1,0:T(8,128)S(1)}, f32[8,128]{1,0:T(8,128)S(1)}, f32[2048,128,8]{1,0,2:T(8,128)}) fusion(f32[2048,128,8]{1,0,2:T(8,128)} %get-tuple-element.47, f32[8,128]{1,0:T(8,128)S(1)} %get-tuple-element.46, pred[128,2048]{0,1:T(8,128)(4,1)S(1)} %iota_compare_fusion, ...), kind=kOutput, calls=%fused_computation.28 | convolution fusion | flops 564129792 | bytes 34623488 | tf_op jit(solution)/shard_map/thd,kd->htk/dot_general | solution.py:53
  89.1 8.0 %exponential_reduce_fusion.2 = (f32[8,128]{1,0:T(8,128)S(1)}, f32[8,128]{1,0:T(8,128)S(1)}, f32[8,128]{1,0:T(8,128)S(1)}) fusion(f32[2048,128,8]{1,0,2:T(8,128)} %get-tuple-element.48, f32[8,128]{1,0:T(8,128)S(1)} %get-tuple-element.37, pred[128,2048]{0,1:T(8,128)(4,1)S(1)} %iota_compare_fusion, f32[8,128]{1,0:T(8,128)S(1)} %get-tuple-element.38, ...), kind=kLoop, calls=%fused_computation.26 | loop fusion | flops 25162752 | bytes 25452544 | tf_op jit(solution)/shard_map/reduce_sum | solution.py:58
  97.2 5.6 %fusion.28 = bf16[2048,128]{0,1:T(8,128)(2,1)S(1)} fusion(bf16[128,4,8,128]{0,3,2,1:T(8,128)(2,1)S(1)} %bitcast.299, f32[2048,128,8]{1,0,2:T(8,128)} %get-tuple-element.48, f32[8,128]{1,0:T(8,128)S(1)} %get-tuple-element.52, pred[128,2048]{0,1:T(8,128)(4,1)S(1)} %iota_compare_fusion), kind=kOutput, calls=%fused_computation.54 | convolution fusion | flops 545521664 | bytes 9441280 | tf_op jit(solution)/shard_map/htk,thd->kd/dot_general | solution.py:81
  102.8 6.1 %fusion.27 = bf16[2048,128]{0,1:T(8,128)(2,1)S(1)} fusion(bf16[128,4,8,128]{0,3,2,1:T(8,128)(2,1)S(1)} %bitcast.300, f32[2048,128,8]{1,0,2:T(8,128)} %get-tuple-element.47, f32[8,128]{1,0:T(8,128)S(1)} %get-tuple-element.53, pred[128,2048]{0,1:T(8,128)(4,1)S(1)} %iota_compare_fusion), kind=kOutput, calls=%fused_computation.53 | convolution fusion | flops 545521664 | bytes 9441280 | tf_op jit(solution)/shard_map/htk,thd->kd/dot_general | solution.py:81
  108.9 2.2 fusion.29
  111.2 2.2 fusion.30
  113.6 2.5 copy.179
  116.2 13.7 %all-gather.6.cloned.1.call-done = bf16[4096,512]{1,0:T(8,128)(2,1)} async-done(((bf16[256,512]{1,0:T(8,128)(2,1)}), bf16[4096,512]{1,0:T(8,128)(2,1)}) %all-gather.6.cloned.1.call-update) | async-done | bytes 4194320 | tf_op jit(solution)/shard_map/all_gather | solution.py:30
  129.9 3.6 fusion.35
  133.5 6.5 %all-reduce.2.cloned.1.call-done = f32[256,2048]{1,0:T(8,128)} async-done(((f32[256,2048]{1,0:T(8,128)}), f32[256,2048]{1,0:T(8,128)}) %all-reduce.2.cloned.1.call-update) | async-done | bytes 2097168 | tf_op jit(solution)/shard_map/psum | solution.py:114
  142.1 60.5 %reduce-scatter.12.cloned.1.call-done = bf16[128,512]{1,0:T(8,128)(2,1)} async-done(((bf16[2048,512]{1,0:T(8,128)(2,1)}), bf16[128,512]{1,0:T(8,128)(2,1)}) %reduce-scatter.12.cloned.1.call-update) | async-done | bytes 131088
  202.6 4.2 fusion.16
  207.0 48.1 %all-gather.8.cloned.1.call-done = bf16[2048,512]{1,0:T(8,128)(2,1)} async-done(((bf16[128,512]{1,0:T(8,128)(2,1)}), bf16[2048,512]{1,0:T(8,128)(2,1)}) %all-gather.8.cloned.1.call-update) | async-done | bytes 2097168 | tf_op jit(solution)/shard_map/all_gather | solution.py:36
  255.1 5.8 %convolution_convert_fusion.6 = bf16[128,8,128]{2,0,1:T(8,128)(2,1)S(1)} fusion(bf16[2048,512]{1,0:T(8,128)(2,1)} %all-gather.8.cloned.1.call-done, f32[2048,128,8]{1,0,2:T(8,128)} %get-tuple-element.48, f32[8,128]{1,0:T(8,128)S(1)} %get-tuple-element.52, pred[128,2048]{0,1:T(8,128)(4,1)S(1)} %iota_compare_fusion), kind=kOutput, calls=%fused_computation.65 | convolution fusion | flops 545390592 | bytes 9441280 | tf_op jit(solution)/shard_map/htk,kd->thd/dot_general | solution.py:62
  260.9 5.6 %convolution_convert_fusion.5 = bf16[128,8,128]{2,0,1:T(8,128)(2,1)S(1)} fusion(bf16[2048,512]{1,0:T(8,128)(2,1)S(1)} %copy-done.17, f32[2048,128,8]{1,0,2:T(8,128)} %copy-done.3, f32[8,128]{1,0:T(8,128)S(1)} %get-tuple-element.51, pred[128,2048]{0,1:T(8,128)(4,1)S(1)} %iota_compare_fusion), kind=kOutput, calls=%fused_computation.64 | convolution fusion | flops 545390592 | bytes 9441280 | tf_op jit(solution)/shard_map/htk,kd->thd/dot_general | solution.py:62
  266.6 2.1 convolution_convert_fusion.4
  268.8 2.9 multiply_reduce_fusion.3
  271.7 4.5 fusion.11
  276.2 3.8 fusion.23
  280.1 4.4 fusion.8
  284.5 3.7 fusion.24
  288.2 3.0 fusion.5
  292.7 3.0 fusion.2
  297.9 2.7 copy.177
  300.7 4.8 %fusion.22 = bf16[1,128,4096]{2,1,0:T(8,128)(2,1)} fusion(bf16[128,512]{1,0:T(8,128)(2,1)S(1)} %copy-done.10, bf16[4096,512]{1,0:T(8,128)(2,1)} %all-gather.6.cloned.1.call-done), kind=kOutput, calls=%fused_computation.40 | convolution fusion | flops 537919488 | bytes 5373952 | tf_op jit(solution)/shard_map/dot_general | solution.py:105
  305.5 3.2 fusion.31
  316.4 64.0 %reduce-scatter.8.cloned.1.call-done = bf16[256,512]{0,1:T(8,128)(2,1)} async-done(((bf16[4096,512]{0,1:T(8,128)(2,1)}), bf16[256,512]{0,1:T(8,128)(2,1)}) %reduce-scatter.8.cloned.1.call-update) | async-done | bytes 262160 | tf_op jit(solution)/shard_map/reduce_scatter | solution.py:102
  382.4 71.2 %reduce-scatter.10.cloned.1.call-done = bf16[128,512]{1,0:T(8,128)(2,1)} async-done(((bf16[2048,512]{1,0:T(8,128)(2,1)}), bf16[128,512]{1,0:T(8,128)(2,1)}) %reduce-scatter.10.cloned.1.call-update) | async-done | bytes 131088
  (107 shorter events, 24.6 us)
Async XLA Ops:
  8.0 121.9 %copy-start = (bf16[1,128,4096]{2,1,0:T(8,128)(2,1)S(1)}, bf16[1,128,4096]{2,1,0:T(8,128)(2,1)}, u32[]{:S(2)}) copy-start(bf16[1,128,4096]{2,1,0:T(8,128)(2,1)} %param.8) | copy-start | bytes 3145732
  8.0 6.3 %copy-start.6 = (bf16[1,128,4096]{2,1,0:T(8,128)(2,1)S(1)}, bf16[1,128,4096]{2,1,0:T(8,128)(2,1)}, u32[]{:S(2)}) copy-start(bf16[1,128,4096]{2,1,0:T(8,128)(2,1)} %param.12) | copy-start | bytes 3145732
  8.0 60.9 %all-gather.12.cloned.1.call-start = ((), (), s32[]{:S(2)}) async-start(), calls=%async_computation.8 | async-start | bytes 2228224 | tf_op jit(solution)/shard_map/all_gather | solution.py:35
  8.8 121.1 %all-gather.6.cloned.1.call-start = ((), (), s32[]{:S(2)}) async-start(), calls=%async_computation.3 | async-start | bytes 4456448 | tf_op jit(solution)/shard_map/all_gather | solution.py:30
  9.5 130.5 %all-reduce.2.cloned.1.call-start = ((), (), s32[]{:S(2)}) async-start(), calls=%async_computation.6 | async-start | bytes 4194304 | tf_op jit(solution)/shard_map/psum | solution.py:114
  12.4 190.2 %reduce-scatter.12.cloned.1.call-start = ((), (), s32[]{:S(2)}) async-start(), calls=%async_computation.10 | async-start | bytes 2228224
  14.3 63.5 %copy-start.4 = (bf16[1,128,4096]{1,2,0:T(8,128)(2,1)}, bf16[1,128,4096]{1,2,0:T(8,128)(2,1)S(1)}, u32[]{:S(2)}) copy-start(bf16[1,128,4096]{1,2,0:T(8,128)(2,1)S(1)} %copy.95) | copy-start | bytes 3145732
  71.4 37.5 %copy-start.3 = (f32[2048,128,8]{1,0,2:T(8,128)}, f32[2048,128,8]{1,0,2:T(8,128)S(1)}, u32[]{:S(2)}) copy-start(f32[2048,128,8]{1,0,2:T(8,128)S(1)} %fusion.40) | copy-start | bytes 25165828
  72.7 38.5 %copy-start.2 = (f32[2048,128,8]{1,0,2:T(8,128)}, f32[2048,128,8]{1,0,2:T(8,128)S(1)}, u32[]{:S(2)}) copy-start(f32[2048,128,8]{1,0,2:T(8,128)S(1)} %fusion.41) | copy-start | bytes 25165828
  89.1 8.1 %copy-start.7 = (bf16[1,128,4096]{1,2,0:T(8,128)(2,1)S(1)}, bf16[1,128,4096]{1,2,0:T(8,128)(2,1)}, u32[]{:S(2)}) copy-start(bf16[1,128,4096]{1,2,0:T(8,128)(2,1)} %copy.108) | copy-start | bytes 3145732
  116.2 138.9 %all-gather.8.cloned.1.call-start = ((), (), s32[]{:S(2)}) async-start(), calls=%async_computation.4 | async-start | bytes 2228224 | tf_op jit(solution)/shard_map/all_gather | solution.py:36
  133.5 167.2 %all-gather.10.cloned.1.call-start = ((), (), s32[]{:S(2)}) async-start(), calls=%async_computation.7 | async-start | bytes 1179648 | tf_op jit(solution)/shard_map/all_gather | solution.py:122
  142.0 238.4 %reduce-scatter.8.cloned.1.call-start = ((), (), s32[]{:S(2)}) async-start(), calls=%async_computation.5 | async-start | bytes 4456448 | tf_op jit(solution)/shard_map/reduce_scatter | solution.py:102
  206.8 246.8 %reduce-scatter.10.cloned.1.call-start = ((), (), s32[]{:S(2)}) async-start(), calls=%async_computation.9 | async-start | bytes 2228224
  255.1 5.8 %copy-start.17 = (bf16[2048,512]{1,0:T(8,128)(2,1)S(1)}, bf16[2048,512]{1,0:T(8,128)(2,1)}, u32[]{:S(2)}) copy-start(bf16[2048,512]{1,0:T(8,128)(2,1)} %all-gather.8.cloned.1.call-done) | copy-start | bytes 6291460
  255.1 11.4 %slice-start = ((s8[8388608]{0:T(1024)(128)(4,1)}), s8[4194304]{0:T(1024)(128)(4,1)S(1)}, s32[]{:S(2)}) async-start(s8[8388608]{0:T(1024)(128)(4,1)} %bitcast.283), calls=%async_computation.11 | async-start | bytes 8388608
  255.1 13.6 %slice-start.6 = ((s8[8388608]{0:T(1024)(128)(4,1)}), s8[4194304]{0:T(1024)(128)(4,1)S(1)}, s32[]{:S(2)}) async-start(s8[8388608]{0:T(1024)(128)(4,1)} %bitcast.321), calls=%async_computation.17 | async-start | bytes 8388608
  260.9 7.8 %copy-start.13 = (bf16[128,8,128]{2,0,1:T(8,128)(2,1)}, bf16[128,8,128]{2,0,1:T(8,128)(2,1)S(1)}, u32[]{:S(2)}) copy-start(bf16[128,8,128]{2,0,1:T(8,128)(2,1)S(1)} %convolution_convert_fusion.6) | copy-start | bytes 786436
  260.9 5.7 %slice-start.1 = ((s8[8388608]{0:T(1024)(128)(4,1)}), s8[4194304]{0:T(1024)(128)(4,1)S(1)}, s32[]{:S(2)}) async-start(s8[8388608]{0:T(1024)(128)(4,1)} %bitcast.283), calls=%async_computation.12 | async-start | bytes 8388608
  260.9 7.8 %slice-start.7 = ((s8[8388608]{0:T(1024)(128)(4,1)}), s8[4194304]{0:T(1024)(128)(4,1)S(1)}, s32[]{:S(2)}) async-start(s8[8388608]{0:T(1024)(128)(4,1)} %bitcast.321), calls=%async_computation.18 | async-start | bytes 8388608
  266.6 5.1 %copy-start.15 = (bf16[128,8,128]{2,0,1:T(8,128)(2,1)}, bf16[128,8,128]{2,0,1:T(8,128)(2,1)S(1)}, u32[]{:S(2)}) copy-start(bf16[128,8,128]{2,0,1:T(8,128)(2,1)S(1)} %convolution_convert_fusion.5) | copy-start | bytes 786436
  268.7 11.3 %slice-start.4 = ((s8[8388608]{0:T(1024)(128)(4,1)}), s8[4194304]{0:T(1024)(128)(4,1)S(1)}, s32[]{:S(2)}) async-start(s8[8388608]{0:T(1024)(128)(4,1)} %bitcast.287), calls=%async_computation.15 | async-start | bytes 8388608
  271.7 8.4 %slice-start.5 = ((s8[8388608]{0:T(1024)(128)(4,1)}), s8[4194304]{0:T(1024)(128)(4,1)S(1)}, s32[]{:S(2)}) async-start(s8[8388608]{0:T(1024)(128)(4,1)} %bitcast.287), calls=%async_computation.16 | async-start | bytes 8388608
  276.2 11.9 %slice-start.2 = ((s8[8388608]{0:T(1024)(128)(4,1)}), s8[4194304]{0:T(1024)(128)(4,1)S(1)}, s32[]{:S(2)}) async-start(s8[8388608]{0:T(1024)(128)(4,1)} %bitcast.285), calls=%async_computation.13 | async-start | bytes 8388608
  280.1 8.1 %slice-start.3 = ((s8[8388608]{0:T(1024)(128)(4,1)}), s8[4194304]{0:T(1024)(128)(4,1)S(1)}, s32[]{:S(2)}) async-start(s8[8388608]{0:T(1024)(128)(4,1)} %bitcast.285), calls=%async_computation.14 | async-start | bytes 8388608
  295.8 4.9 %copy-start.10 = (bf16[128,512]{1,0:T(8,128)(2,1)S(1)}, bf16[128,512]{1,0:T(8,128)(2,1)}, u32[]{:S(2)}) copy-start(bf16[128,512]{1,0:T(8,128)(2,1)} %reduce-scatter.12.cloned.1.call-done) | copy-start | bytes 393220
  300.6 8.1 %copy-start.12 = (bf16[1,2048,512]{2,1,0:T(8,128)(2,1)S(1)}, bf16[1,2048,512]{2,1,0:T(8,128)(2,1)}, u32[]{:S(2)}) copy-start(bf16[1,2048,512]{2,1,0:T(8,128)(2,1)} %all-gather.12.cloned.1.call-done) | copy-start | bytes 6291460
  300.7 8.1 %copy-start.18 = (bf16[8,128,2048]{1,2,0:T(8,128)(2,1)S(1)}, bf16[8,128,2048]{1,2,0:T(8,128)(2,1)}, u32[]{:S(2)}) copy-start(bf16[8,128,2048]{1,2,0:T(8,128)(2,1)} %fusion.8) | copy-start | bytes 12582916
  300.7 8.9 %copy-start.20 = (bf16[8,128,2048]{1,2,0:T(8,128)(2,1)S(1)}, bf16[8,128,2048]{1,2,0:T(8,128)(2,1)}, u32[]{:S(2)}) copy-start(bf16[8,128,2048]{1,2,0:T(8,128)(2,1)} %copy-done.19) | copy-start | bytes 12582916
  305.5 4.9 %copy-start.22 = (bf16[8,128,2048]{1,2,0:T(8,128)(2,1)S(1)}, bf16[8,128,2048]{1,2,0:T(8,128)(2,1)}, u32[]{:S(2)}) copy-start(bf16[8,128,2048]{1,2,0:T(8,128)(2,1)} %copy-done.21) | copy-start | bytes 12582916
  309.6 146.8 %copy-start.1 = (bf16[1,128,4096]{2,1,0:T(8,128)(2,1)S(1)}, bf16[1,128,4096]{2,1,0:T(8,128)(2,1)}, u32[]{:S(2)}) copy-start(bf16[1,128,4096]{2,1,0:T(8,128)(2,1)} %param.8) | copy-start | bytes 3145732
  310.4 145.0 %copy-start.9 = (bf16[256,2048]{1,0:T(8,128)(2,1)S(1)}, bf16[256,2048]{1,0:T(8,128)(2,1)}, u32[]{:S(2)}) copy-start(bf16[256,2048]{1,0:T(8,128)(2,1)} %all-gather.10.cloned.1.call-done) | copy-start | bytes 3145732
  (7 other events, 22.8 us)
Sparse Core Ops, SparseCore 0:
  11.3 57.6 all-gather.11
  71.4 58.4 all-gather.5
  133.8 68.7 reduce-scatter.11
  205.5 49.5 all-gather.7
  257.1 34.3 all-gather.9
  295.3 85.0 reduce-scatter.7
  384.4 69.1 reduce-scatter.9
Sparse Core Ops, SparseCore 1:
  12.5 127.4 all-reduce.1
where the time goes:
time: 473 us; the launch traced here: 464 us
  waiting for transfers between devices  319 us (67%)
  matrix products  97.4 us (21%)
  between operations  16.5 us (3%)
  other arithmetic  15.8 us (3%)
  local copies, waits for them, and re-layouts  15.2 us (3%)
    unnamed x10, waiting for transfers between devices  133 us
    reduce_scatter x1, waiting for transfers between devices, on_device(): lax.psum_scatter((product * proj_scale).astype(jnp.bfloat16), 'fsdp', sca...  64 us
    all_gather x1, waiting for transfers between devices, on_device(): lax.all_gather(keys, 'fsdp', axis=0, tiled=True)  53.3 us
    all_gather x1, waiting for transfers between devices, on_device(): lax.all_gather(values, 'fsdp', axis=0, tiled=True)  48.1 us
    dot_general x4, matrix products, on_device(): jnp.einsum('thd,kd->htk', query_part, key_part, preferred_element_type=jn...  20.1 us
    dot_general x4, matrix products, on_device(): jnp.einsum('htk,kd->thd', probs_low, value_part, preferred_element_type=j...  16.4 us
    dot_general x4, matrix products, on_device(): jnp.einsum('htk,thd->kd', probs_low, grad_part, preferred_element_type=jn...  16.2 us
    unnamed x72, local copies, waits for them, and re-layouts  15.2 us
  transfers between devices with their start and end apart: 8, of which 7 were waited for; matrix products, arithmetic and copies ran while one was open for 27% of the time, Pallas kernels for 0%

commit v1 on v0

--- a/solution.py
+++ b/solution.py
@@ -24,17 +24,17 @@
     score_scale = HD ** (-0.5)
     kv_heads = keys.shape[1] // HD
     group = queries.shape[1] // (kv_heads * HD)
-    columns = tokens
-    value_sum = jnp.dot(
-        columns,
-        lax.all_gather(value_weight, "fsdp", axis=0, tiled=True),
-        preferred_element_type=jnp.float32,
+    key_rows = keys.shape[0]
+    weight_rows = value_weight.shape[0]
+    fsdp_size = lax.axis_size("fsdp")
+    gathered = lax.all_gather(
+        jnp.concatenate([keys, value_weight], axis=0), "fsdp", axis=0, tiled=False
     )
+    keys_all = gathered[:, :key_rows].reshape(fsdp_size * key_rows, keys.shape[1])
+    weight_all = gathered[:, key_rows:].reshape(fsdp_size * weight_rows, value_weight.shape[1])
+    value_sum = jnp.dot(tokens, weight_all, preferred_element_type=jnp.float32)
     values = (value_sum * proj_scale).astype(jnp.bfloat16)
-    keys_all, values_all = (
-        lax.all_gather(keys, "fsdp", axis=0, tiled=True),
-        lax.all_gather(values, "fsdp", axis=0, tiled=True),
-    )
+    values_all = lax.all_gather(values, "fsdp", axis=0, tiled=True)
     length_all = keys_all.shape[0]
     query_pos = lax.axis_index("fsdp") * tok_rows + jnp.arange(tok_rows)
     causal = jnp.arange(length_all)[None, :] <= query_pos[:, None]
@@ -85,37 +85,33 @@
     query_grad = jnp.stack(query_list, axis=1).reshape(tok_rows, queries.shape[1])
     key_term = jnp.concatenate(key_terms, axis=1)
     value_term = jnp.concatenate(value_terms, axis=1)
-    key_sum, value_total = (
-        lax.psum_scatter(
-            key_term.astype(jnp.bfloat16), "fsdp", scatter_dimension=0, tiled=True
-        ).astype(jnp.float32),
-        lax.psum_scatter(
-            value_term.astype(jnp.bfloat16), "fsdp", scatter_dimension=0, tiled=True
-        ).astype(jnp.float32),
-    )
+    kv_width = key_term.shape[1]
+    kv_total = lax.psum_scatter(
+        jnp.concatenate([key_term, value_term], axis=1).astype(jnp.bfloat16),
+        "fsdp",
+        scatter_dimension=0,
+        tiled=True,
+    ).astype(jnp.float32)
+    key_sum = kv_total[:, :kv_width]
+    value_total = kv_total[:, kv_width:]
     key_grad = key_sum.astype(jnp.bfloat16)
     value_grad = value_total.astype(jnp.bfloat16)
-    columns = tokens
     product = lax.dot_general(
-        columns, value_grad, (((0,), (0,)), ((), ())), preferred_element_type=jnp.float32
+        tokens, value_grad, (((0,), (0,)), ((), ())), preferred_element_type=jnp.float32
     )
     weight_grad = lax.psum_scatter(
         (product * proj_scale).astype(jnp.bfloat16), "fsdp", scatter_dimension=0, tiled=True
     ).astype(jnp.float32)
     token_sum = lax.dot_general(
         value_grad,
-        lax.all_gather(value_weight, "fsdp", axis=0, tiled=True),
+        weight_all,
         (((1,), (1,)), ((), ())),
         preferred_element_type=jnp.float32,
     )
     token_grad = (token_sum * proj_scale).astype(jnp.bfloat16)
     replicas = lax.axis_size("replica")
     local_term = frag_local[0].astype(jnp.float32)
-    summed_frag = lax.psum(local_term, "replica")
-    share_cols = frag_global.shape[1]
-    own_sum = lax.dynamic_slice_in_dim(
-        summed_frag, lax.axis_index("replica") * share_cols, share_cols, 1
-    )
+    own_sum = lax.psum_scatter(local_term, "replica", scatter_dimension=1, tiled=True)
     delta = frag_global - own_sum / replicas
     new_momentum = outer_momentum * frag_momentum + delta
     new_global = frag_global - outer_rate * (delta + outer_momentum * new_momentum)

time: 473 us -> 443 us (0.937)
  waiting for transfers between devices: 319 us -> 263 us
  matrix products: 97.4 us -> 115 us
  local copies, waits for them, and re-layouts: 15.2 us -> 26.7 us
    unnamed x10 -> x7, waiting for transfers between devices: 133 us -> 76.9 us
    all_gather x1, waiting for transfers between devices: 0.02 us -> 34 us  [on_device(): lax.all_gather(new_global.astype(jnp.bfloat16), 'replica', axis=1, tiled=...]
    all_gather x3 -> x2, waiting for transfers between devices: 115 us -> 83.3 us  [the longest x1 69.2 us: on_device(): lax.all_gather(jnp.concatenate([keys, value_weight], axis=0), 'fsdp', axi...]
    dot_general x4, matrix products: 14.9 us -> 30.9 us  [on_device(): jnp.einsum('thd,kd->htk', grad_part, value_part, preferred_element_type=j...]
    unnamed x72 -> x61, local copies, waits for them, and re-layouts: 15.2 us -> 22.1 us
    psum x1 -> x0, waiting for transfers between devices: 6.46 us -> none  [on_device(): summed_frag = lax.psum(local_term, 'replica')]
  transfers between devices with their start and end apart: 8 -> 6, of which waited for: 7 -> 5; matrix products, arithmetic and copies ran while one was open for 27% -> 33% of each run, Pallas kernels for 0% -> 0%
where the time goes in v1:
time: 443 us; the launch traced here: 438 us
  waiting for transfers between devices  263 us (59%)
  matrix products  115 us (26%)
  local copies, waits for them, and re-layouts  26.7 us (6%)
  other arithmetic  16.9 us (4%)
  between operations  16.3 us (4%)
    unnamed x7, waiting for transfers between devices  76.9 us
    all_gather x1, waiting for transfers between devices, on_device(): lax.all_gather(jnp.concatenate([keys, value_weight], axis=0), 'fsdp', axi...  69.2 us
    reduce_scatter x1, waiting for transfers between devices, on_device(): lax.psum_scatter((product * proj_scale).astype(jnp.bfloat16), 'fsdp', sca...  68.7 us
    all_gather x1, waiting for transfers between devices, on_device(): lax.all_gather(new_global.astype(jnp.bfloat16), 'replica', axis=1, tiled=...  34 us
    dot_general x4, matrix products, on_device(): jnp.einsum('thd,kd->htk', grad_part, value_part, preferred_element_type=j...  30.9 us
    unnamed x61, local copies, waits for them, and re-layouts  22.1 us
    dot_general x4, matrix products, on_device(): jnp.einsum('thd,kd->htk', query_part, key_part, preferred_element_type=jn...  20 us
    dot_general x4, matrix products, on_device(): jnp.einsum('htk,kd->thd', probs_low, value_part, preferred_element_type=j...  16.6 us
  transfers between devices with their start and end apart: 6, of which 5 were waited for; matrix products, arithmetic and copies ran while one was open for 33% of the time, Pallas kernels for 0%

profile of v1, /device:TPU:1, one launch (start us, length us, event | category | flops | bytes accessed | tf_op | source)
XLA Modules:
  0.0 438.4 jit_solution(1744975181744280646)
XLA Ops:
  10.0 69.2 %all-gather.9.cloned.1.call-done = bf16[6144,512]{1,0:T(8,128)(2,1)} async-done(((bf16[384,512]{1,0:T(8,128)(2,1)}), bf16[6144,512]{1,0:T(8,128)(2,1)}) %all-gather.9.cloned.1.call-update) | async-done | bytes 6291472 | tf_op jit(solution)/shard_map/all_gather | solution.py:30
  79.3 2.7 slice.82
  89.3 2.3 copy.104
  93.4 2.2 fusion.50
  96.9 5.1 %fusion.17 = (f32[8,128]{1,0:T(8,128)S(1)}, f32[2048,128,8]{1,0,2:T(8,128)}) fusion(pred[128,2048]{0,1:T(8,128)(4,1)S(1)} %iota_compare_fusion, bf16[128,4,8,128]{0,3,2,1:T(8,128)(2,1)S(1)} %bitcast.322, bf16[2048,512]{1,0:T(8,128)(2,1)S(1)} %bitcast.307), kind=kOutput, calls=%fused_computation.34 | convolution fusion | flops 543161344 | bytes 9441280 | tf_op jit(solution)/shard_map/thd,kd->htk/dot_general | solution.py:53
  102.0 11.5 %exponential_reduce_fusion.3 = (f32[8,128]{1,0:T(8,128)S(1)}, f32[8,128]{1,0:T(8,128)S(1)}, f32[8,128]{1,0:T(8,128)S(1)}, f32[8,128]{1,0:T(8,128)S(1)}, f32[2048,128,8]{1,0,2:T(8,128)}) fusion(f32[2048,128,8]{1,0,2:T(8,128)} %get-tuple-element.47, f32[8,128]{1,0:T(8,128)S(1)} %get-tuple-element.46, pred[128,2048]{0,1:T(8,128)(4,1)S(1)} %iota_compare_fusion, ...), kind=kOutput, calls=%fused_computation.28 | convolution fusion | flops 564129792 | bytes 34623488 | tf_op jit(solution)/shard_map/thd,kd->htk/dot_general | solution.py:53
  113.5 7.9 %exponential_reduce_fusion.2 = (f32[8,128]{1,0:T(8,128)S(1)}, f32[8,128]{1,0:T(8,128)S(1)}, f32[8,128]{1,0:T(8,128)S(1)}) fusion(f32[2048,128,8]{1,0,2:T(8,128)} %get-tuple-element.48, f32[8,128]{1,0:T(8,128)S(1)} %get-tuple-element.37, pred[128,2048]{0,1:T(8,128)(4,1)S(1)} %iota_compare_fusion, f32[8,128]{1,0:T(8,128)S(1)} %get-tuple-element.38, ...), kind=kLoop, calls=%fused_computation.26 | loop fusion | flops 25162752 | bytes 25452544 | tf_op jit(solution)/shard_map/reduce_sum | solution.py:58
  121.4 14.1 %all-gather.5.cloned.1.call-done = bf16[2048,512]{0,1:T(8,128)(2,1)} async-done(((bf16[128,512]{0,1:T(8,128)(2,1)}), bf16[2048,512]{0,1:T(8,128)(2,1)}) %all-gather.5.cloned.1.call-update) | async-done | bytes 2097168 | tf_op jit(solution)/shard_map/all_gather | solution.py:37
  135.5 5.8 %convolution_convert_fusion.4 = bf16[128,8,128]{2,0,1:T(8,128)(2,1)S(1)} fusion(bf16[2048,512]{0,1:T(8,128)(2,1)} %all-gather.5.cloned.1.call-done, f32[2048,128,8]{1,0,2:T(8,128)} %copy-done.1, f32[8,128]{1,0:T(8,128)S(1)} %get-tuple-element.50, pred[128,2048]{0,1:T(8,128)(4,1)S(1)} %iota_compare_fusion), kind=kOutput, calls=%fused_computation.69 | convolution fusion | flops 545390592 | bytes 9441280 | tf_op jit(solution)/shard_map/htk,kd->thd/dot_general | solution.py:62
  147.0 6.5 %multiply_reduce_fusion.3 = (f32[128,8]{0,1:T(8,128)S(1)}, f32[128,8]{0,1:T(8,128)S(1)}, f32[128,8]{0,1:T(8,128)S(1)}, f32[128,8]{0,1:T(8,128)S(1)}, bf16[128,8,128]{2,0,1:T(8,128)(2,1)}) fusion(bf16[128,4,8,128]{0,3,2,1:T(8,128)(2,1)S(1)} %bitcast.327, bf16[128,8,128]{2,0,1:T(8,128)(2,1)S(1)} %convolution_convert_fusion.4, ...), kind=kOutput, calls=%fused_computation.97 | convolution fusion | flops 547483648 | bytes 11292672 | tf_op jit(solution)/shard_map/htk,kd->thd/dot_general | solution.py:62
  153.6 5.4 %fusion.11 = bf16[8,128,2048]{1,2,0:T(8,128)(2,1)S(1)} fusion(f32[2048,128,8]{1,0,2:T(8,128)} %get-tuple-element.47, f32[8,128]{1,0:T(8,128)S(1)} %bitcast.345, f32[8,128]{1,0:T(8,128)S(1)} %get-tuple-element.53, pred[128,2048]{0,1:T(8,128)(4,1)S(1)} %iota_compare_fusion, bf16[2048,512]{0,1:T(8,128)(2,1)S(1)} %copy-done.21, ...), kind=kOutput, calls=%fused_computation.15 | convolution fusion | flops 551550976 | bytes 13639680 | tf_op jit(solution)/shard_map/thd,kd->htk/dot_general | solution.py:65
  159.0 2.3 fusion.24
  161.3 14.5 %fusion.8 = bf16[8,128,2048]{1,2,0:T(8,128)(2,1)S(1)} fusion(f32[2048,128,8]{1,0,2:T(8,128)S(1)} %bitcast.314, f32[8,128]{1,0:T(8,128)S(1)} %bitcast.344, f32[8,128]{1,0:T(8,128)S(1)} %get-tuple-element.52, pred[128,2048]{0,1:T(8,128)(4,1)S(1)} %iota_compare_fusion, bf16[2048,512]{0,1:T(8,128)(2,1)} %all-gather.5.cloned.1.call-done, ...), kind=kOutput, calls=%fused_computation.11 | convolution fusion | flops 551550976 | bytes 13639680 | tf_op jit(solution)/shard_map/thd,kd->htk/dot_general | solution.py:65
  177.8 2.3 fusion.26
  180.1 5.6 %fusion.5 = bf16[8,128,2048]{1,2,0:T(8,128)(2,1)} fusion(f32[2048,128,8]{1,0,2:T(8,128)S(1)} %copy-done.3, f32[8,128]{1,0:T(8,128)S(1)} %bitcast.343, f32[8,128]{1,0:T(8,128)S(1)} %get-tuple-element.51, pred[128,2048]{0,1:T(8,128)(4,1)S(1)} %iota_compare_fusion, bf16[2048,512]{0,1:T(8,128)(2,1)} %all-gather.5.cloned.1.call-done, ...), kind=kOutput, calls=%fused_computation.7 | convolution fusion | flops 551550976 | bytes 13639680 | tf_op jit(solution)/shard_map/thd,kd->htk/dot_general | solution.py:65
  185.7 4.5 %fusion.28 = bf16[2048,1024]{0,1:T(8,128)(2,1)} fusion(bf16[2048,1024]{0,1:T(8,128)(2,1)} %fusion.26, bf16[8,128,2048]{1,2,0:T(8,128)(2,1)} %fusion.5, bf16[128,4,8,128]{0,3,2,1:T(8,128)(2,1)S(1)} %bitcast.325), kind=kOutput, calls=%fused_computation.54 | convolution fusion | flops 537133056 | bytes 4980736 | tf_op jit(solution)/shard_map/htk,thd->kd/dot_general | solution.py:78
  190.2 5.4 %fusion.2 = bf16[8,128,2048]{1,2,0:T(8,128)(2,1)} fusion(f32[2048,128,8]{1,0,2:T(8,128)S(1)} %bitcast.302, f32[8,128]{1,0:T(8,128)S(1)} %bitcast.342, f32[8,128]{1,0:T(8,128)S(1)} %get-tuple-element.50, pred[128,2048]{0,1:T(8,128)(4,1)S(1)} %iota_compare_fusion, bf16[2048,512]{0,1:T(8,128)(2,1)} %all-gather.5.cloned.1.call-done, ...), kind=kOutput, calls=%fused_computation.3 | convolution fusion | flops 551550976 | bytes 13639680 | tf_op jit(solution)/shard_map/thd,kd->htk/dot_general | solution.py:65
  195.6 4.5 %fusion.30 = bf16[2048,1024]{0,1:T(8,128)(2,1)} fusion(bf16[2048,1024]{0,1:T(8,128)(2,1)} %fusion.28, bf16[8,128,2048]{1,2,0:T(8,128)(2,1)} %fusion.2, bf16[128,4,8,128]{0,3,2,1:T(8,128)(2,1)S(1)} %bitcast.326), kind=kOutput, calls=%fused_computation.56 | convolution fusion | flops 537133056 | bytes 4980736 | tf_op jit(solution)/shard_map/htk,thd->kd/dot_general | solution.py:78
  200.0 6.4 %fusion.32 = bf16[2048,1024]{0,1:T(8,128)(2,1)} fusion(bf16[2048,1024]{0,1:T(8,128)(2,1)} %fusion.30, bf16[128,4,8,128]{0,3,2,1:T(8,128)(2,1)S(1)} %bitcast.332, f32[2048,128,8]{1,0,2:T(8,128)} %get-tuple-element.47, f32[8,128]{1,0:T(8,128)S(1)} %get-tuple-element.53, pred[128,2048]{0,1:T(8,128)(4,1)S(1)} %iota_compare_fusion), kind=kOutput, calls=%fused_computation.58 | convolution fusion | flops 545521664 | bytes 9441280 | tf_op jit(solution)/shard_map/htk,thd->kd/dot_general | solution.py:81
  206.5 3.0 fusion.34
  209.5 3.0 fusion.36
  212.5 3.0 fusion.38
  215.5 6.4 %copy.177 = bf16[2048,1024]{1,0:T(8,128)(2,1)} copy(bf16[2048,1024]{0,1:T(8,128)(2,1)} %fusion.38) | data formatting | bytes 8388608
  224.1 76.8 %reduce-scatter.10.cloned.1.call-done = bf16[128,1024]{1,0:T(8,128)(2,1)} async-done(((bf16[2048,1024]{1,0:T(8,128)(2,1)}), bf16[128,1024]{1,0:T(8,128)(2,1)}) %reduce-scatter.10.cloned.1.call-update) | async-done | bytes 262160
  300.9 4.1 fusion.16
  305.0 34.0 %all-gather.7.cloned.1.call-done = bf16[256,2048]{1,0:T(8,128)(2,1)} async-done(((bf16[256,256]{1,0:T(8,128)(2,1)}), bf16[256,2048]{1,0:T(8,128)(2,1)}) %all-gather.7.cloned.1.call-update) | async-done | bytes 1048592 | tf_op jit(solution)/shard_map/all_gather | solution.py:118
  339.0 2.2 pad_maximum_fusion
  341.2 2.5 copy.133
  343.7 3.1 fusion.42
  346.8 3.6 fusion.41
  354.3 4.6 %fusion.22 = bf16[1,128,4096]{2,1,0:T(8,128)(2,1)} fusion(bf16[4096,512]{1,0:T(8,128)(2,1)} %bitcast.304, bf16[128,1024]{1,0:T(8,128)(2,1)S(1)} %copy-done.15), kind=kOutput, calls=%fused_computation.40 | convolution fusion | flops 537919488 | bytes 5373952 | tf_op jit(solution)/shard_map/dot_general | solution.py:105
  359.0 68.7 %reduce-scatter.6.cloned.1.call-done = bf16[256,512]{0,1:T(8,128)(2,1)} async-done(((bf16[4096,512]{0,1:T(8,128)(2,1)}), bf16[256,512]{0,1:T(8,128)(2,1)}) %reduce-scatter.6.cloned.1.call-update) | async-done | bytes 262160 | tf_op jit(solution)/shard_map/reduce_scatter | solution.py:102
  (91 shorter events, 28.9 us)
Async XLA Ops:
  8.0 76.0 %copy-start = (bf16[1,128,4096]{2,1,0:T(8,128)(2,1)S(1)}, bf16[1,128,4096]{2,1,0:T(8,128)(2,1)}, u32[]{:S(2)}) copy-start(bf16[1,128,4096]{2,1,0:T(8,128)(2,1)} %param.8) | copy-start | bytes 3145732
  8.0 78.1 %copy-start.11 = (bf16[1,256,2048]{2,1,0:T(8,128)(2,1)S(1)}, bf16[1,256,2048]{2,1,0:T(8,128)(2,1)}, u32[]{:S(2)}) copy-start(bf16[1,256,2048]{2,1,0:T(8,128)(2,1)} %param.15) | copy-start | bytes 3145732
  8.0 71.2 %all-gather.9.cloned.1.call-start = ((), (), s32[]{:S(2)}) async-start(), calls=%async_computation.7 | async-start | bytes 6684672 | tf_op jit(solution)/shard_map/all_gather | solution.py:30
  10.0 125.5 %all-gather.5.cloned.1.call-start = ((), (), s32[]{:S(2)}) async-start(), calls=%async_computation.3 | async-start | bytes 2228224 | tf_op jit(solution)/shard_map/all_gather | solution.py:37
  79.3 8.5 %copy-start.12 = (bf16[1,128,4096]{2,1,0:T(8,128)(2,1)S(1)}, bf16[1,128,4096]{2,1,0:T(8,128)(2,1)}, u32[]{:S(2)}) copy-start(bf16[1,128,4096]{2,1,0:T(8,128)(2,1)} %param.9) | copy-start | bytes 3145732
  82.0 2.1 copy-start.4
  86.0 136.0 %reduce-scatter.8.cloned.1.call-start = ((), (), s32[]{:S(2)}) async-start(), calls=%async_computation.5 | async-start | bytes 2359296 | tf_op jit(solution)/shard_map/reduce_scatter | solution.py:114
  87.7 213.1 %reduce-scatter.10.cloned.1.call-start = ((), (), s32[]{:S(2)}) async-start(), calls=%async_computation.8 | async-start | bytes 4456448
  91.6 4.1 copy-start.9
  95.6 17.8 %copy-start.1 = (f32[2048,128,8]{1,0,2:T(8,128)}, f32[2048,128,8]{1,0,2:T(8,128)S(1)}, u32[]{:S(2)}) copy-start(f32[2048,128,8]{1,0,2:T(8,128)S(1)} %fusion.50) | copy-start | bytes 25165828
  96.9 16.6 %copy-start.2 = (f32[2048,128,8]{1,0,2:T(8,128)}, f32[2048,128,8]{1,0,2:T(8,128)S(1)}, u32[]{:S(2)}) copy-start(f32[2048,128,8]{1,0,2:T(8,128)S(1)} %fusion.49) | copy-start | bytes 25165828
  135.5 6.0 %copy-start.3 = (f32[2048,128,8]{1,0,2:T(8,128)S(1)}, f32[2048,128,8]{1,0,2:T(8,128)}, u32[]{:S(2)}) copy-start(f32[2048,128,8]{1,0,2:T(8,128)} %copy-done.2) | copy-start | bytes 25165828
  135.5 6.6 %copy-start.21 = (bf16[2048,512]{0,1:T(8,128)(2,1)S(1)}, bf16[2048,512]{0,1:T(8,128)(2,1)}, u32[]{:S(2)}) copy-start(bf16[2048,512]{0,1:T(8,128)(2,1)} %all-gather.5.cloned.1.call-done) | copy-start | bytes 6291460
  135.5 8.8 %slice-start.2 = ((s8[8388608]{0:T(1024)(128)(4,1)}), s8[4194304]{0:T(1024)(128)(4,1)S(1)}, s32[]{:S(2)}) async-start(s8[8388608]{0:T(1024)(128)(4,1)} %bitcast.313), calls=%async_computation.11 | async-start | bytes 8388608
  141.3 5.7 %copy-start.17 = (bf16[128,8,128]{2,0,1:T(8,128)(2,1)}, bf16[128,8,128]{2,0,1:T(8,128)(2,1)S(1)}, u32[]{:S(2)}) copy-start(bf16[128,8,128]{2,0,1:T(8,128)(2,1)S(1)} %convolution_convert_fusion.4) | copy-start | bytes 786436
  142.1 2.7 slice-start.3
  144.3 9.3 %copy-start.19 = (bf16[128,8,128]{2,0,1:T(8,128)(2,1)}, bf16[128,8,128]{2,0,1:T(8,128)(2,1)S(1)}, u32[]{:S(2)}) copy-start(bf16[128,8,128]{2,0,1:T(8,128)(2,1)S(1)} %convolution_convert_fusion.5) | copy-start | bytes 786436
  144.3 2.7 copy-start.13
  147.0 12.0 %copy-start.20 = (bf16[128,8,128]{2,0,1:T(8,128)(2,1)}, bf16[128,8,128]{2,0,1:T(8,128)(2,1)S(1)}, u32[]{:S(2)}) copy-start(bf16[128,8,128]{2,0,1:T(8,128)(2,1)S(1)} %convolution_convert_fusion.6) | copy-start | bytes 786436
  153.6 5.4 %copy-start.10 = (bf16[1,128,4096]{1,2,0:T(8,128)(2,1)S(1)}, bf16[1,128,4096]{1,2,0:T(8,128)(2,1)}, u32[]{:S(2)}) copy-start(bf16[1,128,4096]{1,2,0:T(8,128)(2,1)} %copy.95) | copy-start | bytes 3145732
  159.0 2.3 copy-start.5
  177.8 12.4 %slice-start = ((s8[8388608]{0:T(1024)(128)(4,1)}), s8[4194304]{0:T(1024)(128)(4,1)S(1)}, s32[]{:S(2)}) async-start(s8[8388608]{0:T(1024)(128)(4,1)} %bitcast.301), calls=%async_computation.9 | async-start | bytes 8388608
  180.1 10.1 %slice-start.1 = ((s8[8388608]{0:T(1024)(128)(4,1)}), s8[4194304]{0:T(1024)(128)(4,1)S(1)}, s32[]{:S(2)}) async-start(s8[8388608]{0:T(1024)(128)(4,1)} %bitcast.301), calls=%async_computation.10 | async-start | bytes 8388608
  215.5 6.6 %copy-start.16 = (f32[256,256]{1,0:T(8,128)S(1)}, f32[256,256]{1,0:T(8,128)}, u32[]{:S(2)}) copy-start(f32[256,256]{1,0:T(8,128)} %param.13) | copy-start | bytes 786436
  222.0 117.0 %all-gather.7.cloned.1.call-start = ((), (), s32[]{:S(2)}) async-start(), calls=%async_computation.6 | async-start | bytes 1179648 | tf_op jit(solution)/shard_map/all_gather | solution.py:118
  224.0 115.0 %copy-start.18 = (bf16[128,8,128]{2,0,1:T(8,128)(2,1)S(1)}, bf16[128,8,128]{2,0,1:T(8,128)(2,1)}, u32[]{:S(2)}) copy-start(bf16[128,8,128]{2,0,1:T(8,128)(2,1)} %copy-done.17) | copy-start | bytes 786436
  224.0 203.6 %reduce-scatter.6.cloned.1.call-start = ((), (), s32[]{:S(2)}) async-start(), calls=%async_computation.4 | async-start | bytes 4456448 | tf_op jit(solution)/shard_map/reduce_scatter | solution.py:102
  343.7 6.7 %copy-start.8 = (bf16[8,128,2048]{1,2,0:T(8,128)(2,1)S(1)}, bf16[8,128,2048]{1,2,0:T(8,128)(2,1)}, u32[]{:S(2)}) copy-start(bf16[8,128,2048]{1,2,0:T(8,128)(2,1)} %copy-done.7) | copy-start | bytes 12582916
  343.7 7.5 %copy-start.6 = (bf16[8,128,2048]{1,2,0:T(8,128)(2,1)S(1)}, bf16[8,128,2048]{1,2,0:T(8,128)(2,1)}, u32[]{:S(2)}) copy-start(bf16[8,128,2048]{1,2,0:T(8,128)(2,1)} %copy-done.5) | copy-start | bytes 12582916
  350.3 3.1 slice-start.4
  350.4 4.0 copy-start.15
  351.9 77.7 %copy-start.14 = (bf16[256,2048]{1,0:T(8,128)(2,1)S(1)}, bf16[256,2048]{1,0:T(8,128)(2,1)}, u32[]{:S(2)}) copy-start(bf16[256,2048]{1,0:T(8,128)(2,1)} %all-gather.7.cloned.1.call-done) | copy-start | bytes 3145732
  (1 other events, 2.0 us)
Sparse Core Ops, SparseCore 0:
  11.8 67.3 all-gather.8
  86.1 49.3 all-gather.4
Sparse Core Ops, SparseCore 1:
  88.9 57.0 reduce-scatter.7
  222.1 78.7 reduce-scatter.9
  302.9 36.1 all-gather.6
  343.1 84.5 reduce-scatter.5
